TPU v7x, 512 devices: a whole 4x8x8 slice. The times are simulated.
512 devices in a mesh: dp: 128 (over z, y, core), proto: 4 (over x).
Axes of the slice: x: 4, y: 8, z: 8, core: 2. Of those that a mesh axis runs over, the one named last changes fastest.
Arguments:
- teacher_emb: bfloat16 [32768, 128], P('dp'), may hold values from -64 to 64
- student_emb: bfloat16 [32768, 128], P('dp'), may hold values from -64 to 64
- prototypes: float32 [32768, 128], P(('dp', 'proto')), may hold values from -0.125 to 0.125
Outputs:
- grad_prototypes: float32 [32768, 128], P(('dp', 'proto'))
- grad_student: float32 [32768, 128], P('dp')
All inputs are finite; a program needn't handle non-finite values.
Results may differ from a plain program's by a relative error of at most 0.012.
The roundings to bfloat16 on the way count: a program that leaves them out, or rounds other values in their place, can miss the bound.
Values may be sent and summed in bfloat16 or wider, within the bound.
No kernel may reach another device: no remote copies, remote signals or barrier semaphores. Data moves between devices by JAX's collectives and lax.ppermute only.
A program may use at most 64 MiB of HBM per device.

v0:
```python
import math
import jax
import jax.numpy as jnp
from jax import lax
from jax.sharding import PartitionSpec as P

ITERS = 3
teacher_temp = 0.07
student_temp = 0.1


def joined(array, axis, combine):
    everything = jax.tree.map(lambda part: lax.all_gather(part, axis), array)
    first = jax.tree.map(lambda part: part[0], everything)

    def hop(k, so_far):
        return combine(so_far, jax.tree.map(lambda part: part[k], everything))

    return lax.fori_loop(1, lax.axis_size(axis), hop, first)


def contract_rows(left, right):
    return lax.dot_general(
        left, right, (((1,), (1,)), ((), ())), preferred_element_type=jnp.float32
    )


def combine_stats(first, second):
    teacher_top = jnp.maximum(first[0], second[0])
    student_top = jnp.maximum(first[1], second[1])
    total = first[2] * jnp.exp(first[1] - student_top) + second[2] * jnp.exp(
        second[1] - student_top
    )
    return (teacher_top, student_top, total)


def per_device(teacher_emb, student_emb, prototypes):
    copies = lax.all_gather(prototypes.astype(jnp.bfloat16), "dp", axis=0, tiled=True)
    rows_here = teacher_emb.shape[0]
    width = teacher_emb.shape[1]
    block = math.gcd(rows_here, 128)
    count_blocks = rows_here // block

    def teacher_block(emb):
        logits = contract_rows(emb, copies)
        top = jnp.max(logits, axis=1)
        return (jnp.exp((logits - top[:, None]) / teacher_temp), top)

    base_local, teacher_local = lax.map(
        teacher_block, teacher_emb.reshape(count_blocks, block, width)
    )
    base_local = base_local.reshape(rows_here, -1)
    teacher_local = teacher_local.reshape(rows_here)

    def student_stats(emb):
        logits = contract_rows(emb, copies) / student_temp
        top = jnp.max(logits, axis=1)
        return (top, jnp.sum(jnp.exp(logits - top[:, None]), axis=1))

    student_local, total_local = lax.map(
        student_stats, student_emb.reshape(count_blocks, block, width)
    )
    student_local = student_local.reshape(rows_here)
    total_local = total_local.reshape(rows_here)
    teacher_top, student_top, total = joined(
        (teacher_local, student_local, total_local), "proto", combine_stats
    )
    shift = jnp.exp((teacher_local - teacher_top) / teacher_temp)
    row_scale = jnp.ones((rows_here,), jnp.float32)
    col_scale = jnp.ones((base_local.shape[1],), jnp.float32)
    for step in range(ITERS):
        partial_cols = jnp.dot(row_scale * shift, base_local, precision=lax.Precision.HIGHEST)
        col_scale = 1.0 / lax.psum(partial_cols, "dp")
        partial_rows = shift * jnp.dot(base_local, col_scale, precision=lax.Precision.HIGHEST)
        row_scale = 1.0 / lax.psum(partial_rows, "proto")
    row_factor = row_scale * shift
    student_factor = jnp.exp(student_local - student_top) / total

    def gradient_block(items):
        emb, plan, factor, local_top, soft_factor = items
        logits = contract_rows(emb, copies) / student_temp
        probs = jnp.exp(logits - local_top[:, None]) * soft_factor[:, None]
        targets = factor[:, None] * plan * col_scale[None, :]
        grads = (probs - targets).astype(jnp.bfloat16)
        return (grads, jnp.dot(grads, copies, preferred_element_type=jnp.float32) / student_temp)

    grad_logits, student_terms = lax.map(
        gradient_block,
        (
            student_emb.reshape(count_blocks, block, width),
            base_local.reshape(count_blocks, block, -1),
            row_factor.reshape(count_blocks, block),
            student_local.reshape(count_blocks, block),
            student_factor.reshape(count_blocks, block),
        ),
    )
    grad_logits = grad_logits.reshape(rows_here, -1)
    grad_student = lax.psum(student_terms.reshape(rows_here, width), "proto")
    grad_prototypes = lax.psum_scatter(
        lax.dot_general(
            grad_logits, student_emb, (((0,), (0,)), ((), ())), preferred_element_type=jnp.float32
        )
        / student_temp,
        "dp",
        scatter_dimension=0,
        tiled=True,
    )
    return (grad_prototypes, grad_student)


def solution(mesh):
    in_specs = (P("dp", None), P("dp", None), P(("dp", "proto"), None))
    out_specs = (P(("dp", "proto"), None), P("dp", None))
    return jax.shard_map(
        per_device, mesh=mesh, in_specs=in_specs, out_specs=out_specs, check_vma=False
    )
```

profile of v0, /device:TPU:2, one launch (start us, length us, event | category | flops | bytes accessed | tf_op | source)
XLA Modules:
  0.0 1962.5 jit_solution(7701246373878074425)
XLA Ops:
  8.7 90.5 %all-gather.5.cloned.1.call-done = bf16[8192,128]{1,0:T(8,128)(2,1)} async-done(((bf16[64,128]{1,0:T(8,128)(2,1)}), bf16[8192,128]{1,0:T(8,128)(2,1)}) %all-gather.5.cloned.1.call-update) | async-done | bytes 2097168 | tf_op jit(solution)/shard_map/all_gather | solution.py:38
  99.2 6.5 while.55
  105.7 7.8 all-gather.1
  113.6 10.0 while.56
  123.6 9.3 all-gather
  132.9 7.0 all-gather.2
  140.1 7.4 fusion.29
  147.5 490.9 %psum.49 = f32[8192]{0:T(1024)S(1)} all-reduce(f32[8192]{0:T(1024)S(1)} %bitcast.163), channel_id=1, replica_groups=mesh['dp'=128,'proto'=4] {'dp'}, use_global_device_ids=true, to_apply=%region_9.10 | all-reduce | flops 8192 | bytes 65536 | tf_op jit(solution)/shard_map/psum | solution.py:73
  638.4 8.9 fusion.30
  647.3 9.9 psum.50
  657.3 7.4 fusion.31
  664.7 490.9 %psum.51 = f32[8192]{0:T(1024)S(1)} all-reduce(f32[8192]{0:T(1024)S(1)} %bitcast.160), channel_id=1, replica_groups=mesh['dp'=128,'proto'=4] {'dp'}, use_global_device_ids=true, to_apply=%region_11.12 | all-reduce | flops 8192 | bytes 65536 | tf_op jit(solution)/shard_map/psum | solution.py:73
  1155.5 8.9 fusion.32
  1164.5 7.7 psum.52
  1172.2 7.4 fusion.33
  1179.6 491.1 %psum.53 = f32[8192]{0:T(1024)S(1)} all-reduce(f32[8192]{0:T(1024)S(1)} %bitcast.162), channel_id=1, replica_groups=mesh['dp'=128,'proto'=4] {'dp'}, use_global_device_ids=true, to_apply=%region_13.14 | all-reduce | flops 8192 | bytes 65536 | tf_op jit(solution)/shard_map/psum | solution.py:73
  1670.7 9.0 fusion.34
  1679.8 9.7 psum.54
  1689.6 11.7 while.58
  1689.6 5.1 bitcast_dynamic-update-slice_fusion.5
  1695.5 5.0 bitcast_dynamic-update-slice_fusion.5
  1702.0 5.4 convolution_multiply_fusion.3
  1707.4 38.4 %all-reduce.2.cloned.1.call-done = f32[256,128]{1,0:T(8,128)} async-done(((f32[256,128]{1,0:T(8,128)}), f32[256,128]{1,0:T(8,128)}) %all-reduce.2.cloned.1.call-update) | async-done | bytes 131088 | tf_op jit(solution)/shard_map/psum | solution.py:98
  1745.8 208.6 %reduce-scatter.2.cloned.1.call-done = f32[64,128]{1,0:T(8,128)} async-done(((f32[8192,128]{1,0:T(8,128)}), f32[64,128]{1,0:T(8,128)}) %reduce-scatter.2.cloned.1.call-update) | async-done | bytes 32784 | tf_op jit(solution)/shard_map/reduce_scatter | solution.py:99
  (72 shorter events, 22.3 us)
Async XLA Ops:
  7.2 92.1 %all-gather.5.cloned.1.call-start = ((), (), s32[]{:S(2)}) async-start(), calls=%async_computation.1 | async-start | bytes 2113536 | tf_op jit(solution)/shard_map/all_gather | solution.py:38
  8.6 1737.2 %all-reduce.2.cloned.1.call-start = ((), (), s32[]{:S(2)}) async-start(), calls=%async_computation.3 | async-start | bytes 262144 | tf_op jit(solution)/shard_map/psum | solution.py:98
  99.2 14.3 copy-start.2
  1670.7 18.8 copy-start
  1670.7 18.8 copy-start.1
  1701.3 0.7 copy-start.3
  1701.9 252.5 %reduce-scatter.2.cloned.1.call-start = ((), (), s32[]{:S(2)}) async-start(), calls=%async_computation.2 | async-start | bytes 4227072 | tf_op jit(solution)/shard_map/reduce_scatter | solution.py:99
Sparse Core Ops, SparseCore 0:
  11.7 87.4 all-gather.4
  1702.1 43.7 all-reduce.1
  1751.4 202.9 reduce-scatter.1
where the time goes:
time: 1960 us
  blocking collectives  1520 us (78%)
  waiting for transfers between devices  338 us (17%)
  matrix products  75.6 us (4%)
    psum x3, blocking collectives, per_device(): col_scale = 1.0 / lax.psum(partial_cols, 'dp')  1470 us
    reduce_scatter x1, waiting for transfers between devices, per_device(): lax.psum_scatter(lax.dot_general(grad_logits, student_emb, (((0,), (0,)),...  209 us
    all_gather x1, waiting for transfers between devices, per_device(): lax.all_gather(prototypes.astype(jnp.bfloat16), 'dp', axis=0, tiled=True)  90.5 us
  transfers between devices with their start and end apart: 3, of which 3 were waited for; matrix products, arithmetic and copies ran while one was open for 0% of the time, Pallas kernels for 0%

commit v1 on v0

--- a/solution.py
+++ b/solution.py
@@ -70,7 +70,7 @@
     col_scale = jnp.ones((base_local.shape[1],), jnp.float32)
     for step in range(ITERS):
         partial_cols = jnp.dot(row_scale * shift, base_local, precision=lax.Precision.HIGHEST)
-        col_scale = 1.0 / lax.psum(partial_cols, "dp")
+        col_scale = 1.0 / jnp.sum(lax.all_gather(partial_cols, "dp"), axis=0)
         partial_rows = shift * jnp.dot(base_local, col_scale, precision=lax.Precision.HIGHEST)
         row_scale = 1.0 / lax.psum(partial_rows, "proto")
     row_factor = row_scale * shift

time: 1960 us -> 761 us (0.39)
  blocking collectives: 1520 us -> 50.1 us
  waiting for transfers between devices: 338 us -> 584 us
    psum x3 -> x0, blocking collectives: 1470 us -> none  [per_device(): col_scale = 1.0 / lax.psum(partial_cols, 'dp')]
    all_gather x0 -> x3, waiting for transfers between devices: none -> 243 us  [per_device(): col_scale = 1.0 / jnp.sum(lax.all_gather(partial_cols, 'dp'), axis=0)]
  transfers between devices with their start and end apart: 3 -> 6, of which waited for: 3 -> 6; matrix products, arithmetic and copies ran while one was open for 0% -> 1% of each run, Pallas kernels for 0% -> 0%
where the time goes in v1:
time: 761 us; the launch traced here: 760 us
  waiting for transfers between devices  584 us (77%)
  matrix products  77.5 us (10%)
  blocking collectives  50.1 us (7%)
  local copies, waits for them, and re-layouts  17.4 us (2%)
  other arithmetic  15.5 us (2%)
  between operations  14.3 us (2%)
    all_gather x3, waiting for transfers between devices, per_device(): col_scale = 1.0 / jnp.sum(lax.all_gather(partial_cols, 'dp'), axis=0)  243 us
    reduce_scatter x1, waiting for transfers between devices, per_device(): lax.psum_scatter(lax.dot_general(grad_logits, student_emb, (((0,), (0,)),...  208 us
    all_gather x1, waiting for transfers between devices, per_device(): lax.all_gather(prototypes.astype(jnp.bfloat16), 'dp', axis=0, tiled=True)  90.6 us
    psum x1, waiting for transfers between devices, per_device(): grad_student = lax.psum(student_terms.reshape(rows_here, width), 'proto')  42 us
    dot_general x3, matrix products, per_device(): jnp.dot(base_local, col_scale, precision=lax.Precision.HIGHEST)  26.8 us
    psum x3, blocking collectives, per_device(): row_scale = 1.0 / lax.psum(partial_rows, 'proto')  26 us
    all_gather x3, blocking collectives, joined(): everything = jax.tree.map(lambda part: lax.all_gather(part, axis), array)  24.1 us
    dot_general x3, matrix products, per_device(): jnp.dot(row_scale * shift, base_local, precision=lax.Precision.HIGHEST)  24.1 us
  transfers between devices with their start and end apart: 6, of which 6 were waited for; matrix products, arithmetic and copies ran while one was open for 1% of the time, Pallas kernels for 0%

profile of v1, /device:TPU:2, one launch (start us, length us, event | category | flops | bytes accessed | tf_op | source)
XLA Modules:
  0.0 759.9 jit_solution(1050147936345062237)
XLA Ops:
  8.7 90.6 %all-gather.11.cloned.1.call-done = bf16[8192,128]{1,0:T(8,128)(2,1)} async-done(((bf16[64,128]{1,0:T(8,128)(2,1)}), bf16[8192,128]{1,0:T(8,128)(2,1)}) %all-gather.11.cloned.1.call-update) | async-done | bytes 2097168 | tf_op jit(solution)/shard_map/all_gather | solution.py:38
  99.2 6.5 while.55
  105.7 7.8 %all-gather.4 = f32[4,1,256]{2,1,0:T(1,128)S(1)} all-gather(f32[1,1,256]{2,1,0:T(1,128)S(1)} %bitcast.175), channel_id=1, replica_groups=mesh['dp'=128,'proto'=4] {'proto'}, dimensions={0}, use_global_device_ids=true | all-gather | bytes 5120 | tf_op jit(solution)/shard_map/all_gather | solution.py:13
  113.6 10.0 %while.56 = (s32[]{:T(128)}, f32[2,128,8192]{2,1,0:T(8,128)}, f32[2,128]{1,0:T(2,128)S(1)}, bf16[2,128,128]{2,1,0:T(8,128)(2,1)S(1)}, bf16[8192,128]{1,0:T(8,128)(2,1)}, /*index=5*/s32[]{:T(128)}, s32[]{:T(128)}) while((s32[]{:T(128)}, f32[2,128,8192]{2,1,0:T(8,128)}, f32[2,128]{1,0:T(2,128)S(1)}, bf16[2,128,128]{2,1,0:T(8,128)(2,1)S(1)}, ...), condition=%wide.region_2.3_spmd, body=%wide.region_0.2_spmd.sunk | while | flops 271581056 | bytes 14715477 | solution.py:49
  123.6 9.3 %all-gather.3 = f32[4,1,256]{2,1,0:T(1,128)S(1)} all-gather(f32[1,1,256]{2,1,0:T(1,128)S(1)} %bitcast.184), channel_id=1, replica_groups=mesh['dp'=128,'proto'=4] {'proto'}, dimensions={0}, use_global_device_ids=true | all-gather | bytes 5120 | tf_op jit(solution)/shard_map/all_gather | solution.py:13
  132.9 7.0 all-gather.5
  140.1 8.0 %fusion.29 = f32[1,8192]{1,0:T(1,128)} fusion(f32[256,1]{0,1:T(1,128)S(1)} %bitcast.170, f32[256,8192]{1,0:T(8,128)} %bitcast.148), kind=kOutput, calls=%fused_computation.55 | convolution fusion | flops 25165824 | bytes 8422400 | tf_op jit(solution)/shard_map/dot_general | solution.py:72
  148.2 81.1 %all-gather.13.cloned.1.call-done = f32[1048576]{0:T(1024)} async-done(((f32[8192]{0:T(1024)}), f32[1048576]{0:T(1024)}) %all-gather.13.cloned.1.call-update) | async-done | bytes 4194320 | tf_op jit(solution)/shard_map/all_gather | solution.py:73
  236.7 8.9 %fusion.30 = f32[1,256]{1,0:T(1,128)S(1)} fusion(f32[256,8192]{1,0:T(8,128)} %bitcast.149, f32[8192,1]{0,1:T(1,128)S(1)} %bitcast.162), kind=kOutput, calls=%fused_computation.56 | convolution fusion | flops 25165824 | bytes 8422400 | tf_op jit(solution)/shard_map/dot_general | solution.py:74
  245.6 8.8 %psum.28 = f32[256]{0:T(256)S(1)} all-reduce(f32[256]{0:T(256)S(1)} %mul.66), channel_id=1, replica_groups=mesh['dp'=128,'proto'=4] {'proto'}, use_global_device_ids=true, to_apply=%region_10.11 | all-reduce | flops 256 | bytes 2048 | tf_op jit(solution)/shard_map/psum | solution.py:75
  254.4 8.0 %fusion.31 = f32[1,8192]{1,0:T(1,128)} fusion(f32[256,1]{0,1:T(1,128)S(1)} %bitcast.180, f32[256,8192]{1,0:T(8,128)} %bitcast.150), kind=kOutput, calls=%fused_computation.57 | convolution fusion | flops 25165824 | bytes 8422400 | tf_op jit(solution)/shard_map/dot_general | solution.py:72
  262.5 81.3 %all-gather.15.cloned.1.call-done = f32[1048576]{0:T(1024)} async-done(((f32[8192]{0:T(1024)}), f32[1048576]{0:T(1024)}) %all-gather.15.cloned.1.call-update) | async-done | bytes 4194320 | tf_op jit(solution)/shard_map/all_gather | solution.py:73
  351.2 8.9 %fusion.32 = f32[1,256]{1,0:T(1,128)S(1)} fusion(f32[256,8192]{1,0:T(8,128)} %bitcast.151, f32[8192,1]{0,1:T(1,128)S(1)} %bitcast.163), kind=kOutput, calls=%fused_computation.58 | convolution fusion | flops 25165824 | bytes 8422400 | tf_op jit(solution)/shard_map/dot_general | solution.py:74
  360.1 8.6 %psum.29 = f32[256]{0:T(256)S(1)} all-reduce(f32[256]{0:T(256)S(1)} %mul.68), channel_id=1, replica_groups=mesh['dp'=128,'proto'=4] {'proto'}, use_global_device_ids=true, to_apply=%region_12.13 | all-reduce | flops 256 | bytes 2048 | tf_op jit(solution)/shard_map/psum | solution.py:75
  368.8 8.0 %fusion.33 = f32[1,8192]{1,0:T(1,128)} fusion(f32[256,1]{0,1:T(1,128)S(1)} %bitcast.182, f32[256,8192]{1,0:T(8,128)} %bitcast.152), kind=kOutput, calls=%fused_computation.59 | convolution fusion | flops 25165824 | bytes 8422400 | tf_op jit(solution)/shard_map/dot_general | solution.py:72
  377.1 81.0 %all-gather.17.cloned.1.call-done = f32[1048576]{0:T(1024)} async-done(((f32[8192]{0:T(1024)}), f32[1048576]{0:T(1024)}) %all-gather.17.cloned.1.call-update) | async-done | bytes 4194320 | tf_op jit(solution)/shard_map/all_gather | solution.py:73
  465.5 9.0 %fusion.34 = f32[1,256]{1,0:T(1,128)S(1)} fusion(f32[256,8192]{1,0:T(8,128)} %bitcast.153, f32[8192,1]{0,1:T(1,128)S(1)} %bitcast.158), kind=kOutput, calls=%fused_computation.60 | convolution fusion | flops 25165824 | bytes 8422400 | tf_op jit(solution)/shard_map/dot_general | solution.py:74
  474.6 8.6 %psum.30 = f32[256]{0:T(256)S(1)} all-reduce(f32[256]{0:T(256)S(1)} %mul.70), channel_id=1, replica_groups=mesh['dp'=128,'proto'=4] {'proto'}, use_global_device_ids=true, to_apply=%region_14.15 | all-reduce | flops 256 | bytes 2048 | tf_op jit(solution)/shard_map/psum | solution.py:75
  483.2 11.7 %while.58 = (s32[]{:T(128)}, bf16[2,128,8192]{2,1,0:T(8,128)(2,1)}, f32[2,128,128]{2,1,0:T(8,128)S(1)}, bf16[2,128,128]{2,1,0:T(8,128)(2,1)S(1)}, bf16[8192,128]...) while((s32[]{:T(128)}, bf16[2,128,8192]{2,1,0:T(8,128)(2,1)}, ...), condition=%wide.region_16.17_spmd, body=%wide.region_15.16_spmd.sunk | while | flops 544227328 | bytes 14816889 | solution.py:87
  483.3 5.1 bitcast_dynamic-update-slice_fusion.5
  489.1 5.0 bitcast_dynamic-update-slice_fusion.5
  495.6 5.4 convolution_multiply_fusion.3
  501.1 42.0 %all-reduce.2.cloned.1.call-done = f32[256,128]{1,0:T(8,128)} async-done(((f32[256,128]{1,0:T(8,128)}), f32[256,128]{1,0:T(8,128)}) %all-reduce.2.cloned.1.call-update) | async-done | bytes 131088 | tf_op jit(solution)/shard_map/psum | solution.py:98
  543.1 208.4 %reduce-scatter.2.cloned.1.call-done = f32[64,128]{1,0:T(8,128)} async-done(((f32[8192,128]{1,0:T(8,128)}), f32[64,128]{1,0:T(8,128)}) %reduce-scatter.2.cloned.1.call-update) | async-done | bytes 32784 | tf_op jit(solution)/shard_map/reduce_scatter | solution.py:99
  (84 shorter events, 44.8 us)
Async XLA Ops:
  7.2 92.1 %all-gather.11.cloned.1.call-start = ((), (), s32[]{:S(2)}) async-start(), calls=%async_computation.1 | async-start | bytes 2113536 | tf_op jit(solution)/shard_map/all_gather | solution.py:38
  8.6 220.7 %all-gather.13.cloned.1.call-start = ((), (), s32[]{:S(2)}) async-start(), calls=%async_computation.4 | async-start | bytes 4227072 | tf_op jit(solution)/shard_map/all_gather | solution.py:73
  99.2 14.3 %copy-start.2 = (bf16[256,128]{1,0:T(8,128)(2,1)S(1)}, bf16[256,128]{1,0:T(8,128)(2,1)}, u32[]{:S(2)}) copy-start(bf16[256,128]{1,0:T(8,128)(2,1)} %param.11) | copy-start | bytes 196612
  148.2 195.6 %all-gather.15.cloned.1.call-start = ((), (), s32[]{:S(2)}) async-start(), calls=%async_computation.5 | async-start | bytes 4227072 | tf_op jit(solution)/shard_map/all_gather | solution.py:73
  262.5 195.7 %all-gather.17.cloned.1.call-start = ((), (), s32[]{:S(2)}) async-start(), calls=%async_computation.6 | async-start | bytes 4227072 | tf_op jit(solution)/shard_map/all_gather | solution.py:73
  376.8 166.3 %all-reduce.2.cloned.1.call-start = ((), (), s32[]{:S(2)}) async-start(), calls=%async_computation.3 | async-start | bytes 262144 | tf_op jit(solution)/shard_map/psum | solution.py:98
  465.5 17.7 %copy-start = (bf16[8192,128]{1,0:T(8,128)(2,1)S(1)}, bf16[8192,128]{1,0:T(8,128)(2,1)}, u32[]{:S(2)}) copy-start(bf16[8192,128]{1,0:T(8,128)(2,1)} %get-tuple-element.669) | copy-start | bytes 6291460
  465.5 17.7 %copy-start.1 = (bf16[2,128,128]{2,1,0:T(8,128)(2,1)S(1)}, bf16[2,128,128]{2,1,0:T(8,128)(2,1)}, u32[]{:S(2)}) copy-start(bf16[2,128,128]{2,1,0:T(8,128)(2,1)} %get-tuple-element.675) | copy-start | bytes 196612
  494.9 0.7 copy-start.3
  495.6 255.9 %reduce-scatter.2.cloned.1.call-start = ((), (), s32[]{:S(2)}) async-start(), calls=%async_computation.2 | async-start | bytes 4227072 | tf_op jit(solution)/shard_map/reduce_scatter | solution.py:99
Sparse Core Ops, SparseCore 0:
  11.7 87.4 all-gather.10
  148.3 80.9 all-gather.12
  262.6 81.1 all-gather.14
  376.9 81.1 all-gather.16
  495.7 47.3 all-reduce.1
  548.6 202.8 reduce-scatter.1

commit v2 on v0

--- a/solution.py
+++ b/solution.py
@@ -35,7 +35,12 @@
 
 
 def per_device(teacher_emb, student_emb, prototypes):
-    copies = lax.all_gather(prototypes.astype(jnp.bfloat16), "dp", axis=0, tiled=True)
+    copies = jnp.concatenate(
+        lax.all_to_all(
+            jnp.stack([prototypes.astype(jnp.bfloat16)] * lax.axis_size("dp")), "dp", 0, 0
+        ),
+        axis=0,
+    )
     rows_here = teacher_emb.shape[0]
     width = teacher_emb.shape[1]
     block = math.gcd(rows_here, 128)

time: 1960 us -> 1880 us (0.959)
  waiting for transfers between devices: 338 us -> 244 us
    all_gather x1 -> x0, waiting for transfers between devices: 90.5 us -> none  [per_device(): lax.all_gather(prototypes.astype(jnp.bfloat16), 'dp', axis=0, tiled=True)]
    all_to_all x0 -> x1, waiting for transfers between devices: none -> 52.5 us  [per_device(): lax.all_to_all(jnp.stack([prototypes.astype(jnp.bfloat16)] * lax.axis_siz...]
    reduce_scatter x1, waiting for transfers between devices: 209 us -> 156 us  [per_device(): lax.psum_scatter(lax.dot_general(grad_logits, student_emb, (((0,), (0,)),...]
where the time goes in v2:
time: 1880 us
  blocking collectives  1520 us (81%)
  waiting for transfers between devices  244 us (13%)
  matrix products  69 us (4%)
    psum x3, blocking collectives, per_device(): col_scale = 1.0 / lax.psum(partial_cols, 'dp')  1470 us
    reduce_scatter x1, waiting for transfers between devices, per_device(): lax.psum_scatter(lax.dot_general(grad_logits, student_emb, (((0,), (0,)),...  156 us
    all_to_all x1, waiting for transfers between devices, per_device(): lax.all_to_all(jnp.stack([prototypes.astype(jnp.bfloat16)] * lax.axis_siz...  52.5 us
  transfers between devices with their start and end apart: 3, of which 3 were waited for; matrix products, arithmetic and copies ran while one was open for 0% of the time, Pallas kernels for 0%

profile of v2, /device:TPU:2, one launch (start us, length us, event | category | flops | bytes accessed | tf_op | source)
XLA Modules:
  0.0 1883.4 jit_solution(12072566992711255181)
XLA Ops:
  10.7 17.8 all-to-all-start
  28.6 52.5 %all-to-all-done = bf16[128,64,128]{2,1,0:T(8,128)(2,1)S(1)} async-done(((bf16[128,64,128]{2,1,0:T(8,128)(2,1)}), bf16[128,64,128]{2,1,0:T(8,128)(2,1)S(1)}, u32[]{:S(2)}, u32[]{:S(2)}) %all-to-all-start) | async-done | bytes 2097184 | tf_op jit(solution)/shard_map/all_to_all | solution.py:39
  84.3 7.8 all-gather.1
  92.2 6.8 while.56
  99.0 9.4 all-gather
  108.4 7.0 all-gather.2
  115.6 7.4 fusion.29
  123.0 491.0 %psum.49 = f32[8192]{0:T(1024)S(1)} all-reduce(f32[8192]{0:T(1024)S(1)} %bitcast.165), channel_id=1, replica_groups=mesh['dp'=128,'proto'=4] {'dp'}, use_global_device_ids=true, to_apply=%region_9.10 | all-reduce | flops 8192 | bytes 65536 | tf_op jit(solution)/shard_map/psum | solution.py:78
  614.1 8.9 fusion.30
  623.0 9.7 psum.50
  632.7 7.4 fusion.31
  640.2 490.9 %psum.51 = f32[8192]{0:T(1024)S(1)} all-reduce(f32[8192]{0:T(1024)S(1)} %bitcast.162), channel_id=1, replica_groups=mesh['dp'=128,'proto'=4] {'dp'}, use_global_device_ids=true, to_apply=%region_11.12 | all-reduce | flops 8192 | bytes 65536 | tf_op jit(solution)/shard_map/psum | solution.py:78
  1131.0 8.9 fusion.32
  1139.9 8.0 psum.52
  1147.9 7.4 fusion.33
  1155.3 490.9 %psum.53 = f32[8192]{0:T(1024)S(1)} all-reduce(f32[8192]{0:T(1024)S(1)} %bitcast.164), channel_id=1, replica_groups=mesh['dp'=128,'proto'=4] {'dp'}, use_global_device_ids=true, to_apply=%region_13.14 | all-reduce | flops 8192 | bytes 65536 | tf_op jit(solution)/shard_map/psum | solution.py:78
  1646.2 8.9 fusion.34
  1655.1 9.7 psum.54
  1664.9 11.7 while.58
  1664.9 5.1 bitcast_dynamic-update-slice_fusion.5
  1670.8 5.0 bitcast_dynamic-update-slice_fusion.5
  1677.3 5.4 convolution_multiply_fusion.3
  1682.7 35.5 %all-reduce.2.cloned.1.call-done = f32[256,128]{1,0:T(8,128)} async-done(((f32[256,128]{1,0:T(8,128)}), f32[256,128]{1,0:T(8,128)}) %all-reduce.2.cloned.1.call-update) | async-done | bytes 131088 | tf_op jit(solution)/shard_map/psum | solution.py:103
  1718.3 156.1 %reduce-scatter.2.cloned.1.call-done = f32[64,128]{1,0:T(8,128)} async-done(((f32[8192,128]{1,0:T(8,128)}), f32[64,128]{1,0:T(8,128)}) %reduce-scatter.2.cloned.1.call-update) | async-done | bytes 32784 | tf_op jit(solution)/shard_map/reduce_scatter | solution.py:104
  (70 shorter events, 20.3 us)
Async XLA Ops:
  8.0 73.1 %copy-start = (bf16[256,128]{1,0:T(8,128)(2,1)S(1)}, bf16[256,128]{1,0:T(8,128)(2,1)}, u32[]{:S(2)}) copy-start(bf16[256,128]{1,0:T(8,128)(2,1)} %param.12) | copy-start | bytes 196612
  10.7 70.4 %all-to-all-start = ((bf16[128,64,128]{2,1,0:T(8,128)(2,1)}), bf16[128,64,128]{2,1,0:T(8,128)(2,1)S(1)}, u32[]{:S(2)}, u32[]{:S(2)}) async-start(bf16[128,64,128]{2,1,0:T(8,128)(2,1)} %stack.2), calls=%async_computation | async-start | bytes 4194304 | tf_op jit(solution)/shard_map/all_to_all | solution.py:39
  28.5 1689.8 %all-reduce.2.cloned.1.call-start = ((), (), s32[]{:S(2)}) async-start(), calls=%async_computation.3 | async-start | bytes 262144 | tf_op jit(solution)/shard_map/psum | solution.py:103
  81.1 11.1 copy-start.1
  1676.5 0.7 copy-start.2
  1677.2 197.1 %reduce-scatter.2.cloned.1.call-start = ((), (), s32[]{:S(2)}) async-start(), calls=%async_computation.2 | async-start | bytes 4227072 | tf_op jit(solution)/shard_map/reduce_scatter | solution.py:104
Sparse Core Ops, SparseCore 0:
  1677.3 40.8 all-reduce.1
Sparse Core Ops, SparseCore 1:
  1682.8 191.5 reduce-scatter.1
